TPU v7x, 128 devices: a whole 4x4x4 slice. The times are simulated.
128 devices in a mesh: item: 4 (over y_hi, core), row: 8 (over y_lo, x), col: 4 (over z).
Axes of the slice: x: 4, y: 4 (y_hi: 2, y_lo: 2; y = y_hi * 2 + y_lo), z: 4, core: 2. Of those that a mesh axis runs over, the one named last changes fastest.
Arguments:
- latents: bfloat16 [64, 64, 4, 2432], P('row', 'col', 'item'), may hold values from -6 to 6
- prompt_tokens: bfloat16 [160, 4, 2432], P('row', 'item'), may hold values from -6 to 6
- text_count: int32 [4], P('item'), may hold values from 1 to 160, as said below
- step_index: int32 [4], P('item'), may hold values from 0 to 27
- step_table: float32 [28, 6, 2432], replicated, may hold values from -3 to 3
- item_mod: float32 [4, 6, 2432], P('item'), may hold values from -3 to 3
- w_qkv: bfloat16 [2432, 3, 1536], P(None, None, 'col'), may hold values from -1 to 1
- w_kv_text: bfloat16 [2432, 2, 1536], P(None, None, 'col'), may hold values from -0.125 to 0.125
- q_gain: float32 [64], replicated, may hold values from 0.5 to 6.5
- k_gain: float32 [64], replicated, may hold values from 0.5 to 6.5
- w_out: bfloat16 [1536, 2432], P('col'), may hold values from -0.15625 to 0.15625
- w_up: bfloat16 [2432, 9728], P(None, ('item', 'col')), may hold values from -0.125 to 0.125
- w_down: bfloat16 [9728, 2432], P(('item', 'col')), may hold values from -0.0625 to 0.0625
Outputs:
- updated: bfloat16 [64, 64, 4, 2432], P('row', 'col', 'item')
Inputs may be any that keep to these rules, and one draw needn't show every extreme that they name: `text_count`: some item has all 160 text tokens live.
All inputs are finite; a program needn't handle non-finite values.
Results may differ from a plain program's by a relative error of at most 0.022.
The roundings to bfloat16 on the way count: a program that leaves them out, or rounds other values in their place, can miss the bound.
Values may be sent and summed in bfloat16 or wider, within the bound.
No kernel may reach another device: no remote copies, remote signals or barrier semaphores. Data moves between devices by JAX's collectives and lax.ppermute only.
A program may use at most 192 MiB of HBM per device.

v0:
```python
import jax
import jax.numpy as jnp
from jax import lax
from jax.sharding import PartitionSpec as P

epsilon = 1e-06


def layer_norm(values):
    values = values.astype(jnp.float32)
    center = values - jnp.mean(values, axis=-1, keepdims=True)
    variance = jnp.mean(center * center, axis=-1, keepdims=True)
    return center * lax.rsqrt(variance + epsilon)


def rms_heads(values, gain):
    return values * lax.rsqrt(jnp.mean(values * values, axis=-1, keepdims=True) + epsilon) * gain


def local(
    latents,
    prompt_tokens,
    text_count,
    step_index,
    step_table,
    item_mod,
    w_qkv,
    w_kv_text,
    q_gain,
    k_gain,
    w_out,
    w_up,
    w_down,
):
    grid_rows, grid_cols, local_items, model_width = latents.shape
    own_rows = grid_rows * grid_cols
    tokens = latents.reshape(own_rows, local_items, model_width)
    wide_up, wide_down = (w_up, w_down)
    chosen = (
        step_index[:, None] == jnp.arange(step_table.shape[0], dtype=jnp.int32)[None, :]
    ).astype(jnp.float32)
    modulation = (
        jnp.einsum("is,sjd->ijd", chosen, step_table, precision=lax.Precision.HIGHEST) + item_mod
    )
    strip_rows = lax.all_gather(tokens, "col", axis=0, tiled=True)
    strip_len = strip_rows.shape[0]
    normed_one = (layer_norm(strip_rows) * (1.0 + modulation[:, 1]) + modulation[:, 0]).astype(
        jnp.bfloat16
    )
    projected = jnp.einsum("sid,dce->csie", normed_one, w_qkv, preferred_element_type=jnp.float32)
    head_cols = w_qkv.shape[2]
    local_heads = head_cols // 64
    query = rms_heads(projected[0].reshape(strip_len, local_items, local_heads, 64), q_gain).astype(
        jnp.bfloat16
    )
    key_img = (
        rms_heads(projected[1].reshape(strip_len, local_items, local_heads, 64), k_gain)
        .astype(jnp.bfloat16)
        .reshape(strip_len, local_items, head_cols)
    )
    value_img = projected[2].astype(jnp.bfloat16)
    text_len = prompt_tokens.shape[0]
    text_normed = layer_norm(prompt_tokens).astype(jnp.bfloat16)
    text_proj = jnp.einsum(
        "tid,dce->ctie", text_normed, w_kv_text, preferred_element_type=jnp.float32
    )
    text_key = (
        rms_heads(text_proj[0].reshape(text_len, local_items, local_heads, 64), k_gain)
        .astype(jnp.bfloat16)
        .reshape(text_len, local_items, head_cols)
    )
    text_value = text_proj[1].astype(jnp.bfloat16)
    position = lax.axis_index("row") * text_len + jnp.arange(text_len, dtype=jnp.int32)
    text_bias = jnp.where(position[:, None] < text_count[None, :], 0.0, -jnp.inf).astype(
        jnp.float32
    )
    run_max = jnp.full((local_items, local_heads, strip_len), -jnp.inf, jnp.float32)
    run_sum = jnp.zeros((local_items, local_heads, strip_len), jnp.float32)
    accum = jnp.zeros((local_items, local_heads, strip_len, 64), jnp.float32)
    key_piece = lax.all_gather(key_img, "row", axis=0, tiled=True)
    value_piece = lax.all_gather(value_img, "row", axis=0, tiled=True)
    tkey_piece = lax.all_gather(text_key, "row", axis=0, tiled=True)
    tvalue_piece = lax.all_gather(text_value, "row", axis=0, tiled=True)
    bias_piece = lax.all_gather(text_bias.astype(jnp.bfloat16), "row", axis=0, tiled=True).astype(
        jnp.float32
    )
    key_piece = key_piece.reshape(key_piece.shape[0], local_items, local_heads, 64)
    value_piece = value_piece.reshape(value_piece.shape[0], local_items, local_heads, 64)
    tkey_piece = tkey_piece.reshape(tkey_piece.shape[0], local_items, local_heads, 64)
    tvalue_piece = tvalue_piece.reshape(tvalue_piece.shape[0], local_items, local_heads, 64)
    score_img = (
        jnp.einsum("sihd,kihd->ihsk", query, key_piece, preferred_element_type=jnp.float32) * 0.125
    )
    score_txt = (
        jnp.einsum("sihd,kihd->ihsk", query, tkey_piece, preferred_element_type=jnp.float32) * 0.125
    )
    score_txt = score_txt + jnp.transpose(bias_piece)[:, None, None, :]
    new_max = jnp.maximum(
        run_max, jnp.maximum(jnp.max(score_img, axis=-1), jnp.max(score_txt, axis=-1))
    )
    rescale = jnp.exp(run_max - new_max)
    prob_img = jnp.exp(score_img - new_max[..., None])
    prob_txt = jnp.exp(score_txt - new_max[..., None])
    run_sum = run_sum * rescale + jnp.sum(prob_img, axis=-1) + jnp.sum(prob_txt, axis=-1)
    accum = accum * rescale[..., None]
    accum = accum + jnp.einsum(
        "ihsk,kihd->ihsd",
        prob_img.astype(jnp.bfloat16),
        value_piece,
        preferred_element_type=jnp.float32,
    )
    accum = accum + jnp.einsum(
        "ihsk,kihd->ihsd",
        prob_txt.astype(jnp.bfloat16),
        tvalue_piece,
        preferred_element_type=jnp.float32,
    )
    run_max, run_sum, accum = (new_max, run_sum, accum)
    heads_out = (accum / run_sum[..., None]).astype(jnp.bfloat16)
    attended = jnp.transpose(heads_out, (2, 0, 1, 3)).reshape(strip_len, local_items, head_cols)
    block_rows = attended
    attn_out = lax.psum_scatter(
        jnp.einsum("sie,ed->sid", block_rows, w_out, preferred_element_type=jnp.float32).astype(
            jnp.bfloat16
        ),
        "col",
        scatter_dimension=0,
        tiled=True,
    ).astype(jnp.float32)
    residual = (tokens.astype(jnp.float32) + modulation[:, 2] * attn_out).astype(jnp.bfloat16)
    normed_two = (layer_norm(residual) * (1.0 + modulation[:, 4]) + modulation[:, 3]).astype(
        jnp.bfloat16
    )
    residual, flat_rows = (residual, normed_two.reshape(own_rows * local_items, model_width))
    hidden = jax.nn.gelu(
        jnp.dot(
            lax.all_gather(flat_rows, ("item", "col"), axis=0, tiled=True),
            wide_up,
            preferred_element_type=jnp.float32,
        ),
        approximate=True,
    ).astype(jnp.bfloat16)
    block_rows = hidden
    mlp_sum = lax.psum_scatter(
        jnp.dot(block_rows, wide_down, preferred_element_type=jnp.float32).astype(jnp.bfloat16),
        ("item", "col"),
        scatter_dimension=0,
        tiled=True,
    ).astype(jnp.float32)
    mlp_sum = mlp_sum.reshape(own_rows, local_items, model_width)
    updated = (residual.astype(jnp.float32) + modulation[:, 5] * mlp_sum).astype(jnp.bfloat16)
    return updated.reshape(grid_rows, grid_cols, local_items, model_width)


def solution(mesh):
    placed = (
        P("row", "col", "item", None),
        P("row", "item", None),
        P("item"),
        P("item"),
        P(),
        P("item", None, None),
        P(None, None, "col"),
        P(None, None, "col"),
        P(),
        P(),
        P("col", None),
        P(None, ("item", "col")),
        P(("item", "col"), None),
    )
    return jax.shard_map(
        local, mesh=mesh, in_specs=placed, out_specs=P("row", "col", "item", None), check_vma=False
    )
```

profile of v0, /device:TPU:1, one launch (start us, length us, event | category | flops | bytes accessed | tf_op | source)
XLA Modules:
  0.0 471.7 jit_solution(10957942517682658492)
XLA Ops:
  6.5 0.0 copy-start
  6.5 0.7 all-gather.8.cloned.1.call-update
  7.3 0.0 all-gather.10.cloned.1.call-start
  8.1 2.2 fusion.77
  10.3 0.7 mul.292
  11.0 0.1 mul.293
  11.1 0.9 reshape_add_fusion
  11.9 0.2 slice_reduce_fusion.1
  12.1 34.5 %all-gather.8.cloned.1.call-done = bf16[512,1,2432]{2,0,1:T(8,128)(2,1)} async-done(((bf16[128,1,2432]{2,0,1:T(8,128)(2,1)}), bf16[512,1,2432]{2,0,1:T(8,128)(2,1)}) %all-gather.8.cloned.1.call-update) | async-done | bytes 2490384 | tf_op jit(solution)/shard_map/all_gather | solution.py:45
  46.6 2.3 convert_reduce_fusion
  48.9 0.2 copy-done.1
  49.0 0.8 fusion.8
  49.8 6.1 %fusion.39 = f32[3,512,1,384]{1,3,0,2:T(8,128)S(1)} fusion(bf16[2432,3,384]{2,0,1:T(8,128)(2,1)} %param.19, bf16[512,1,2432]{2,0,1:T(8,128)(2,1)S(1)} %copy-done.1, f32[2432]{0:T(1024)S(1)} %get-tuple-element.8, f32[2432]{0:T(1024)S(1)} %get-tuple-element.9, f32[512]{0:T(512)S(1)} %add_rsqrt_fusion.3, f32[512]{0:T(512)S(1)} %broadcast_multiply_fusion), kind=kOutput, calls=%fused_computation.45 | convolution fusion | flops 2876375040 | bytes 10476544 | tf_op jit(solution)/shard_map/sid,dce->csie/dot_general | solution.py:50
  56.0 1.4 copy-done.4
  57.4 1.6 slice_multiply_fusion.2
  59.0 1.2 reduce_sum.102
  60.3 0.1 mul.289
  60.3 2.1 fusion.64
  62.4 0.0 all-gather.10.cloned.1.call-update
  62.4 0.0 copy-start.9
  62.4 0.0 all-gather.12.cloned.1.call-start
  62.5 0.1 convert_reduce_fusion.2
  62.6 0.2 fusion.67
  62.9 2.7 fusion.56
  65.6 0.1 mul.302
  65.7 0.1 reduce_sum.105
  65.8 0.1 mul.303
  65.9 0.1 mul.304
  66.0 25.3 %all_gather.23 = bf16[160,1,384]{2,1,0:T(2,128)(2,1)S(1)} all-gather(bf16[20,1,384]{2,1,0:T(2,128)(2,1)S(1)} %copy.26), channel_id=1, replica_groups=mesh['item'=4,'row'=8,'col'=4] {'row'}, dimensions={0}, use_global_device_ids=true | all-gather | bytes 138240 | tf_op jit(solution)/shard_map/all_gather | solution.py:82
  91.3 0.2 copy.27
  92.2 0.6 dynamic-slice
  93.4 0.2 dynamic-update-slice
  93.6 16.2 %all-reduce = bf16[160]{0:T(256)(128)(2,1)S(1)} all-reduce(bf16[160]{0:T(256)(128)(2,1)S(1)} %dynamic-update-slice), channel_id=1, replica_groups=mesh['item'=4,'row'=8,'col'=4] {'row'}, use_global_device_ids=true, to_apply=%add | all-reduce | flops 160 | bytes 640
  109.8 22.0 %all-gather.1 = bf16[1,160,1,384]{3,2,0,1:T(2,128)(2,1)S(1)} all-gather(bf16[1,20,1,384]{3,2,0,1:T(2,128)(2,1)S(1)} %copy.28), channel_id=3, replica_groups=mesh['item'=4,'row'=8,'col'=4] {'row'}, dimensions={1}, use_global_device_ids=true | all-gather | bytes 138240 | tf_op jit(solution)/shard_map/all_gather | solution.py:83
  131.8 0.9 copy.29
  132.7 1.9 slice.74
  134.7 1.2 reduce_sum.101
  135.9 0.0 all-gather.12.cloned.1.call-update
  135.9 0.2 reduce-scatter.3.cloned.1.call-start
  136.2 2.9 fusion.38
  139.1 21.7 %multiply_reduce_fusion = (f32[6,512]{1,0:T(8,128)S(1)}, f32[6,512,4096]{2,1,0:T(8,128)}) fusion(bf16[4096,6,64]{0,2,1:T(8,128)(2,1)} %bitcast.91, f32[512,6,64]{0,2,1:T(8,128)} %bitcast.90, f32[64]{0:T(128)S(1)} %copy-done.8, f32[512,6]{0,1:T(8,128)S(1)} %add_rsqrt_fusion.1), kind=kOutput, calls=%fused_computation.1 | convolution fusion | flops 1636365312 | bytes 54288640 | tf_op jit(solution)/shard_map/sihd,kihd->ihsk/dot_general | solution.py:92
  160.7 2.1 fusion.42
  162.8 20.8 %fusion = f32[6,512]{1,0:T(8,128)S(1)} fusion(f32[6,512,4096]{2,1,0:T(8,128)} %get-tuple-element.19, f32[6,512]{1,0:T(8,128)S(1)} %get-tuple-element.14), kind=kLoop, calls=%fused_computation.2 | loop fusion | flops 37745664 | bytes 50356224 | tf_op jit(solution)/shard_map/reduce_sum | solution.py:104
  183.6 4.3 all-gather.12.cloned.1.call-done
  187.9 19.8 %fusion.47 = f32[6,512,64]{1,2,0:T(8,128)S(1)} fusion(bf16[4096,6,64]{0,2,1:T(8,128)(2,1)} %bitcast.95, f32[6,512,4096]{2,1,0:T(8,128)} %get-tuple-element.19, f32[6,512]{1,0:T(8,128)S(1)} %get-tuple-element.14, f32[6,512]{1,0:T(8,128)S(1)} %get-tuple-element.13), kind=kOutput, calls=%fused_computation.52 | convolution fusion | flops 1648558080 | bytes 54288384 | tf_op jit(solution)/shard_map/ihsk,kihd->ihsd/dot_general | solution.py:106
  207.7 0.0 copy-start.5
  207.7 0.6 fusion.50
  208.4 0.8 copy-done.5
  209.2 3.0 fusion.20
  212.2 0.0 reduce-scatter.3.cloned.1.call-update
  212.2 0.0 all-gather.14.cloned.1.call-start
  212.3 39.9 %reduce-scatter.3.cloned.1.call-done = bf16[128,1,2432]{2,0,1:T(8,128)(2,1)} async-done(((bf16[512,1,2432]{2,0,1:T(8,128)(2,1)}), bf16[128,1,2432]{2,0,1:T(8,128)(2,1)}) %reduce-scatter.3.cloned.1.call-update) | async-done | bytes 622608 | tf_op jit(solution)/shard_map/reduce_scatter | solution.py:122
  252.2 1.6 convert_reduce_fusion.1
  253.7 0.0 copy-start.2
  253.8 0.3 fusion.51
  254.1 0.5 copy-done.2
  254.6 1.3 fusion.54
  255.9 0.0 all-gather.14.cloned.1.call-update
  255.9 0.3 reduce-scatter.5.cloned.1.call-start
  256.2 79.7 %all-gather.14.cloned.1.call-done = bf16[2048,1,2432]{2,0,1:T(8,128)(2,1)} async-done(((bf16[128,1,2432]{2,0,1:T(8,128)(2,1)}), bf16[2048,1,2432]{2,0,1:T(8,128)(2,1)}) %all-gather.14.cloned.1.call-update) | async-done | bytes 9961488 | tf_op jit(solution)/shard_map/all_gather | solution.py:137
  335.8 20.5 %convolution_convert_fusion = bf16[2048,2432]{1,0:T(8,128)(2,1)} fusion(bf16[608,2432]{1,0:T(8,128)(2,1)S(1)} %copy-done, bf16[2432,608]{0,1:T(8,128)(2,1)} %param.24, bf16[2048,1,2432]{2,0,1:T(8,128)(2,1)} %all-gather.14.cloned.1.call-done), kind=kOutput, calls=%fused_computation.5 | convolution fusion | flops 12129337344 | bytes 25837568 | tf_op jit(solution)/shard_map/dot_general | solution.py:145
  356.3 0.0 reduce-scatter.5.cloned.1.call-update
  356.3 106.2 %reduce-scatter.5.cloned.1.call-done = bf16[128,2432]{1,0:T(8,128)(2,1)} async-done(((bf16[2048,2432]{1,0:T(8,128)(2,1)}), bf16[128,2432]{1,0:T(8,128)(2,1)}) %reduce-scatter.5.cloned.1.call-update) | async-done | bytes 622608 | tf_op jit(solution)/shard_map/reduce_scatter | solution.py:144
  462.6 2.3 fusion.55
  (34 shorter events, 0.2 us)
Async XLA Ops:
  6.5 329.3 %copy-start = (bf16[608,2432]{1,0:T(8,128)(2,1)S(1)}, bf16[608,2432]{1,0:T(8,128)(2,1)}, u32[]{:S(2)}) copy-start(bf16[608,2432]{1,0:T(8,128)(2,1)} %param.25) | copy-start | bytes 8871940
  6.5 40.1 %all-gather.8.cloned.1.call-start = ((), (), s32[]{:S(2)}) async-start(), calls=%async_computation.2 | async-start | bytes 3112960 | tf_op jit(solution)/shard_map/all_gather | solution.py:45
  7.3 131.8 %all-gather.10.cloned.1.call-start = ((), (), s32[]{:S(2)}) async-start(), calls=%async_computation.3 | async-start | bytes 3538944 | tf_op jit(solution)/shard_map/all_gather | solution.py:80
  46.6 2.5 copy-start.1
  56.0 1.4 copy-start.4
  59.0 3.5 copy-start.6
  62.4 29.8 %copy-start.9 = (u32[128]{0:T(128)S(1)}, u32[128]{0:T(128)}, u32[]{:S(2)}) copy-start(u32[128]{0:T(128)} %constant.56) | copy-start | bytes 1540
  62.4 125.4 %all-gather.12.cloned.1.call-start = ((), (), s32[]{:S(2)}) async-start(), calls=%async_computation.6 | async-start | bytes 3538944 | tf_op jit(solution)/shard_map/all_gather | solution.py:81
  65.6 70.6 %copy-start.8 = (f32[64]{0:T(128)S(1)}, f32[64]{0:T(128)}, u32[]{:S(2)}) copy-start(f32[64]{0:T(128)} %param.21) | copy-start | bytes 772
  135.9 116.3 %reduce-scatter.3.cloned.1.call-start = ((), (), s32[]{:S(2)}) async-start(), calls=%async_computation.4 | async-start | bytes 3112960 | tf_op jit(solution)/shard_map/reduce_scatter | solution.py:122
  187.8 19.9 %copy-start.3 = (f32[6,512,160]{1,2,0:T(8,128)S(1)}, f32[6,512,160]{1,2,0:T(8,128)}, u32[]{:S(2)}) copy-start(f32[6,512,160]{1,2,0:T(8,128)} %get-tuple-element.21) | copy-start | bytes 5898244
  187.8 19.9 %copy-start.7 = (bf16[1,160,1,384]{1,3,2,0:T(8,128)(2,1)S(1)}, bf16[1,160,1,384]{1,3,2,0:T(8,128)(2,1)}, u32[]{:S(2)}) copy-start(bf16[1,160,1,384]{1,3,2,0:T(8,128)(2,1)} %copy.29) | copy-start | bytes 368644
  207.7 1.5 copy-start.5
  212.2 123.6 %all-gather.14.cloned.1.call-start = ((), (), s32[]{:S(2)}) async-start(), calls=%async_computation.7 | async-start | bytes 10584064 | tf_op jit(solution)/shard_map/all_gather | solution.py:137
  253.7 0.8 copy-start.2
  255.9 206.7 %reduce-scatter.5.cloned.1.call-start = ((), (), s32[]{:S(2)}) async-start(), calls=%async_computation.5 | async-start | bytes 10584064 | tf_op jit(solution)/shard_map/reduce_scatter | solution.py:144
Sparse Core Ops, SparseCore 0:
  9.0 37.5 all-gather.7
  62.5 44.3 all-gather.9
  136.0 51.7 all-gather.11
  212.3 39.7 reduce-scatter.2
  256.0 79.7 all-gather.13
  356.5 106.0 reduce-scatter.4
where the time goes:
time: 473 us; the launch traced here: 472 us
  waiting for transfers between devices  265 us (56%)
  matrix products  79.6 us (17%)
  blocking collectives  63.5 us (13%)
  other arithmetic  39 us (8%)
  between operations  15.7 us (3%)
  local copies, waits for them, and re-layouts  7.92 us (2%)
    reduce_scatter x1, waiting for transfers between devices, local(): lax.psum_scatter(jnp.dot(block_rows, wide_down, preferred_element_type=jn...  106 us
    all_gather x1, waiting for transfers between devices, local(): lax.all_gather(flat_rows, ('item', 'col'), axis=0, tiled=True)  79.7 us
    reduce_scatter x1, waiting for transfers between devices, local(): lax.psum_scatter(jnp.einsum('sie,ed->sid', block_rows, w_out, preferred_e...  39.9 us
    all_gather x1, waiting for transfers between devices, local(): strip_rows = lax.all_gather(tokens, 'col', axis=0, tiled=True)  34.5 us
    all_gather x1, blocking collectives, local(): tkey_piece = lax.all_gather(text_key, 'row', axis=0, tiled=True)  25.3 us
    all_gather x1, blocking collectives, local(): tvalue_piece = lax.all_gather(text_value, 'row', axis=0, tiled=True)  22 us
    dot_general x1, matrix products, local(): jnp.einsum('sihd,kihd->ihsk', query, key_piece, preferred_element_type=jn...  21.7 us
    reduce_sum x1, other arithmetic, local(): jnp.sum(prob_img, axis=-1)  20.8 us
  transfers between devices with their start and end apart: 6, of which 5 were waited for; matrix products, arithmetic and copies ran while one was open for 13% of the time, Pallas kernels for 0%

commit v1 on v0

--- a/solution.py
+++ b/solution.py
@@ -2,6 +2,7 @@
 import jax.numpy as jnp
 from jax import lax
 from jax.sharding import PartitionSpec as P
+from jax.lax import all_to_all, axis_size
 
 epsilon = 1e-06
 
@@ -32,6 +33,15 @@
     w_up,
     w_down,
 ):
+
+    def read_run(view):
+        queue = []
+        for _ in range(axis_size("col")):
+            queue.append(view)
+        q_next = jnp.concatenate(queue, axis=0)
+        now = all_to_all(q_next, axis_name="col", split_axis=0, concat_axis=0, tiled=True)
+        return now
+
     grid_rows, grid_cols, local_items, model_width = latents.shape
     own_rows = grid_rows * grid_cols
     tokens = latents.reshape(own_rows, local_items, model_width)
@@ -42,7 +52,7 @@
     modulation = (
         jnp.einsum("is,sjd->ijd", chosen, step_table, precision=lax.Precision.HIGHEST) + item_mod
     )
-    strip_rows = lax.all_gather(tokens, "col", axis=0, tiled=True)
+    strip_rows = read_run(tokens)
     strip_len = strip_rows.shape[0]
     normed_one = (layer_norm(strip_rows) * (1.0 + modulation[:, 1]) + modulation[:, 0]).astype(
         jnp.bfloat16

time: 473 us -> 489 us (1.034)
  local copies, waits for them, and re-layouts: 7.92 us -> 18.2 us
  other arithmetic: 39 us -> 47.3 us
  waiting for transfers between devices: 265 us -> 257 us
  starting transfers between devices: 0.61 us -> 6.56 us
    all_gather x1 -> x0, waiting for transfers between devices: 34.5 us -> none  [local(): strip_rows = lax.all_gather(tokens, 'col', axis=0, tiled=True)]
    all_to_all x0 -> x1, waiting for transfers between devices: none -> 26.8 us  [read_run(): all_to_all(q_next, axis_name='col', split_axis=0, concat_axis=0, tiled=True)]
    unnamed x23 -> x29, local copies, waits for them, and re-layouts: 3.77 us -> 14.2 us
    concatenate x0 -> x2, other arithmetic: none -> 8.51 us  [read_run(): q_next = jnp.concatenate(queue, axis=0)]
    all_to_all x0 -> x1, starting transfers between devices: none -> 5.99 us  [read_run(): all_to_all(q_next, axis_name='col', split_axis=0, concat_axis=0, tiled=True)]
  transfers between devices with their start and end apart: 6 -> 6, of which waited for: 5 -> 5; matrix products, arithmetic and copies ran while one was open for 13% -> 12% of each run, Pallas kernels for 0% -> 0%
where the time goes in v1:
time: 489 us; the launch traced here: 488 us
  waiting for transfers between devices  257 us (53%)
  matrix products  79.6 us (16%)
  blocking collectives  63.8 us (13%)
  other arithmetic  47.3 us (10%)
  local copies, waits for them, and re-layouts  18.2 us (4%)
  between operations  15.3 us (3%)
  starting transfers between devices  6.56 us (1%)
    reduce_scatter x1, waiting for transfers between devices, local(): lax.psum_scatter(jnp.dot(block_rows, wide_down, preferred_element_type=jn...  106 us
    all_gather x1, waiting for transfers between devices, local(): lax.all_gather(flat_rows, ('item', 'col'), axis=0, tiled=True)  79.7 us
    reduce_scatter x1, waiting for transfers between devices, local(): lax.psum_scatter(jnp.einsum('sie,ed->sid', block_rows, w_out, preferred_e...  39.8 us
    all_to_all x1, waiting for transfers between devices, read_run(): all_to_all(q_next, axis_name='col', split_axis=0, concat_axis=0, tiled=True)  26.8 us
    all_gather x1, blocking collectives, local(): tkey_piece = lax.all_gather(text_key, 'row', axis=0, tiled=True)  25.2 us
    all_gather x1, blocking collectives, local(): tvalue_piece = lax.all_gather(text_value, 'row', axis=0, tiled=True)  22.3 us
    dot_general x1, matrix products, local(): jnp.einsum('sihd,kihd->ihsk', query, key_piece, preferred_element_type=jn...  21.7 us
    reduce_sum x1, other arithmetic, local(): jnp.sum(prob_img, axis=-1)  20.8 us
  transfers between devices with their start and end apart: 6, of which 5 were waited for; matrix products, arithmetic and copies ran while one was open for 12% of the time, Pallas kernels for 0%

profile of v1, /device:TPU:1, one launch (start us, length us, event | category | flops | bytes accessed | tf_op | source)
XLA Modules:
  0.0 487.8 jit_solution(7789156698399843077)
XLA Ops:
  6.5 3.6 pad_maximum_fusion
  10.1 0.5 broadcast.277
  10.6 4.9 %reduce.32 = bf16[512,2432]{1,0:T(8,128)(2,1)} reduce(bf16[512,1,2432]{2,0,1:T(8,128)(2,1)} %pad_maximum_fusion, bf16[]{:T(256)} %broadcast.277), dimensions={1}, to_apply=%copy.32.reduce_sub_computation | reduce | bytes 4980738 | tf_op jit(solution)/shard_map/concatenate | solution.py:41
  15.6 4.2 reshape.515
  19.8 6.0 %all-to-all-start = ((bf16[4,2,155648]{2,1,0:T(2,128)(2,1)}), bf16[4,2,155648]{2,1,0:T(2,128)(2,1)}, u32[]{:S(2)}, u32[]{:S(2)}) async-start(bf16[4,2,155648]{2,1,0:T(2,128)(2,1)} %reshape.515), calls=%async_computation | async-start | bytes 4980736 | tf_op jit(solution)/shard_map/all_to_all | solution.py:42
  26.4 2.2 fusion.77
  28.7 0.1 mul.293
  28.8 0.1 reshape_add_fusion
  28.8 0.2 slice_reduce_fusion.1
  29.0 26.8 %all-to-all-done = bf16[4,2,155648]{2,1,0:T(2,128)(2,1)} async-done(((bf16[4,2,155648]{2,1,0:T(2,128)(2,1)}), bf16[4,2,155648]{2,1,0:T(2,128)(2,1)}, u32[]{:S(2)}, u32[]{:S(2)}) %all-to-all-start) | async-done | bytes 2490400 | tf_op jit(solution)/shard_map/all_to_all | solution.py:42
  55.7 5.4 %reshape.516 = bf16[512,1,2432]{2,1,0:T(2,128)(2,1)} reshape(bf16[4,2,155648]{2,1,0:T(2,128)(2,1)} %all-to-all-done) | data formatting | bytes 4980736
  61.1 2.9 convert_reduce_fusion
  64.0 1.0 copy-done.1
  65.0 0.8 fusion.8
  65.8 6.1 %fusion.39 = f32[3,512,1,384]{1,3,0,2:T(8,128)S(1)} fusion(bf16[2432,3,384]{2,0,1:T(8,128)(2,1)} %param.19, f32[2432]{0:T(1024)S(1)} %get-tuple-element.8, f32[2432]{0:T(1024)S(1)} %get-tuple-element.9, f32[512]{0:T(512)S(1)} %add_rsqrt_fusion.3, f32[512]{0:T(512)S(1)} %broadcast_multiply_fusion, bf16[512,1,2432]{2,1,0:T(2,128)(2,1)S(1)} %copy-done.1), kind=kOutput, calls=%fused_computation.46 | convolution fusion | flops 2876375040 | bytes 10476544 | tf_op jit(solution)/shard_map/sid,dce->csie/dot_general | solution.py:60
  71.9 1.4 copy-done.4
  73.3 1.6 slice_multiply_fusion.2
  74.9 1.2 reduce_sum.102
  76.2 0.1 mul.289
  76.3 2.1 fusion.64
  78.4 0.0 all-gather.7.cloned.1.call-update
  78.4 0.0 copy-start.11
  78.4 0.0 all-gather.9.cloned.1.call-start
  78.5 0.1 convert_reduce_fusion.2
  78.6 0.2 fusion.67
  78.8 2.7 fusion.56
  81.6 0.1 mul.302
  81.7 0.1 reduce_sum.105
  81.8 0.1 mul.303
  81.9 0.1 mul.304
  82.0 25.2 %all_gather.19 = bf16[160,1,384]{2,1,0:T(2,128)(2,1)S(1)} all-gather(bf16[20,1,384]{2,1,0:T(2,128)(2,1)S(1)} %copy.36), channel_id=1, replica_groups=mesh['item'=4,'row'=8,'col'=4] {'row'}, dimensions={0}, use_global_device_ids=true | all-gather | bytes 138240 | tf_op jit(solution)/shard_map/all_gather | solution.py:92
  107.2 0.2 copy.37
  108.1 0.6 dynamic-slice
  109.2 0.2 dynamic-update-slice
  109.5 16.3 %all-reduce = bf16[160]{0:T(256)(128)(2,1)S(1)} all-reduce(bf16[160]{0:T(256)(128)(2,1)S(1)} %dynamic-update-slice), channel_id=1, replica_groups=mesh['item'=4,'row'=8,'col'=4] {'row'}, use_global_device_ids=true, to_apply=%add | all-reduce | flops 160 | bytes 640
  125.8 22.3 %all-gather.1 = bf16[1,160,1,384]{3,2,0,1:T(2,128)(2,1)S(1)} all-gather(bf16[1,20,1,384]{3,2,0,1:T(2,128)(2,1)S(1)} %copy.38), channel_id=3, replica_groups=mesh['item'=4,'row'=8,'col'=4] {'row'}, dimensions={1}, use_global_device_ids=true | all-gather | bytes 138240 | tf_op jit(solution)/shard_map/all_gather | solution.py:93
  148.1 0.9 copy.39
  149.0 1.9 slice.74
  150.9 1.2 reduce_sum.101
  152.2 0.0 all-gather.9.cloned.1.call-update
  152.2 0.2 reduce-scatter.3.cloned.1.call-start
  152.4 2.9 fusion.38
  155.3 21.7 %multiply_reduce_fusion = (f32[6,512]{1,0:T(8,128)S(1)}, f32[6,512,4096]{2,1,0:T(8,128)}) fusion(bf16[4096,6,64]{0,2,1:T(8,128)(2,1)} %bitcast.91, f32[512,6,64]{0,2,1:T(8,128)} %bitcast.90, f32[64]{0:T(128)S(1)} %copy-done.9, f32[512,6]{0,1:T(8,128)S(1)} %add_rsqrt_fusion.1), kind=kOutput, calls=%fused_computation.1 | convolution fusion | flops 1636365312 | bytes 54288640 | tf_op jit(solution)/shard_map/sihd,kihd->ihsk/dot_general | solution.py:102
  177.0 2.0 fusion.42
  179.0 20.8 %fusion = f32[6,512]{1,0:T(8,128)S(1)} fusion(f32[6,512,4096]{2,1,0:T(8,128)} %get-tuple-element.19, f32[6,512]{1,0:T(8,128)S(1)} %get-tuple-element.14), kind=kLoop, calls=%fused_computation.2 | loop fusion | flops 37745664 | bytes 50356224 | tf_op jit(solution)/shard_map/reduce_sum | solution.py:114
  199.8 4.6 all-gather.9.cloned.1.call-done
  204.4 19.8 %fusion.47 = f32[6,512,64]{1,2,0:T(8,128)S(1)} fusion(bf16[4096,6,64]{0,2,1:T(8,128)(2,1)} %bitcast.95, f32[6,512,4096]{2,1,0:T(8,128)} %get-tuple-element.19, f32[6,512]{1,0:T(8,128)S(1)} %get-tuple-element.14, f32[6,512]{1,0:T(8,128)S(1)} %get-tuple-element.13), kind=kOutput, calls=%fused_computation.53 | convolution fusion | flops 1648558080 | bytes 54288384 | tf_op jit(solution)/shard_map/ihsk,kihd->ihsd/dot_general | solution.py:116
  224.3 0.6 fusion.50
  225.0 0.8 copy-done.5
  225.8 3.0 fusion.20
  228.8 0.0 reduce-scatter.3.cloned.1.call-update
  228.8 0.0 all-gather.11.cloned.1.call-start
  228.9 39.8 %reduce-scatter.3.cloned.1.call-done = bf16[128,1,2432]{2,0,1:T(8,128)(2,1)} async-done(((bf16[512,1,2432]{2,0,1:T(8,128)(2,1)}), bf16[128,1,2432]{2,0,1:T(8,128)(2,1)}) %reduce-scatter.3.cloned.1.call-update) | async-done | bytes 622608 | tf_op jit(solution)/shard_map/reduce_scatter | solution.py:132
  268.7 1.6 convert_reduce_fusion.1
  270.3 0.3 fusion.51
  270.6 0.5 copy-done.2
  271.1 1.3 fusion.54
  272.4 0.0 all-gather.11.cloned.1.call-update
  272.4 0.3 reduce-scatter.5.cloned.1.call-start
  272.7 79.7 %all-gather.11.cloned.1.call-done = bf16[2048,1,2432]{2,0,1:T(8,128)(2,1)} async-done(((bf16[128,1,2432]{2,0,1:T(8,128)(2,1)}), bf16[2048,1,2432]{2,0,1:T(8,128)(2,1)}) %all-gather.11.cloned.1.call-update) | async-done | bytes 9961488 | tf_op jit(solution)/shard_map/all_gather | solution.py:147
  352.3 20.5 %convolution_convert_fusion = bf16[2048,2432]{1,0:T(8,128)(2,1)} fusion(bf16[608,2432]{1,0:T(8,128)(2,1)S(1)} %copy-done, bf16[2432,608]{0,1:T(8,128)(2,1)} %param.24, bf16[2048,1,2432]{2,0,1:T(8,128)(2,1)} %all-gather.11.cloned.1.call-done), kind=kOutput, calls=%fused_computation.5 | convolution fusion | flops 12129337344 | bytes 25837568 | tf_op jit(solution)/shard_map/dot_general | solution.py:155
  372.9 0.0 reduce-scatter.5.cloned.1.call-update
  372.9 106.1 %reduce-scatter.5.cloned.1.call-done = bf16[128,2432]{1,0:T(8,128)(2,1)} async-done(((bf16[2048,2432]{1,0:T(8,128)(2,1)}), bf16[128,2432]{1,0:T(8,128)(2,1)}) %reduce-scatter.5.cloned.1.call-update) | async-done | bytes 622608 | tf_op jit(solution)/shard_map/reduce_scatter | solution.py:154
  479.0 2.3 fusion.55
  (42 shorter events, 0.2 us)
Async XLA Ops:
  6.5 345.8 %copy-start = (bf16[608,2432]{1,0:T(8,128)(2,1)S(1)}, bf16[608,2432]{1,0:T(8,128)(2,1)}, u32[]{:S(2)}) copy-start(bf16[608,2432]{1,0:T(8,128)(2,1)} %param.25) | copy-start | bytes 8871940
  19.8 8.9 %copy-start.10 = (f32[64]{0:T(128)S(1)}, f32[64]{0:T(128)}, u32[]{:S(2)}) copy-start(f32[64]{0:T(128)} %param.22) | copy-start | bytes 772
  19.8 9.0 %copy-start.8 = (f32[1,6,2432]{2,0,1:T(1,128)S(1)}, f32[1,6,2432]{2,0,1:T(1,128)}, u32[]{:S(2)}) copy-start(f32[1,6,2432]{2,0,1:T(1,128)} %param.18) | copy-start | bytes 175108
  19.8 36.0 %all-to-all-start = ((bf16[4,2,155648]{2,1,0:T(2,128)(2,1)}), bf16[4,2,155648]{2,1,0:T(2,128)(2,1)}, u32[]{:S(2)}, u32[]{:S(2)}) async-start(bf16[4,2,155648]{2,1,0:T(2,128)(2,1)} %reshape.515), calls=%async_computation | async-start | bytes 4980736 | tf_op jit(solution)/shard_map/all_to_all | solution.py:42
  25.8 129.6 %all-gather.7.cloned.1.call-start = ((), (), s32[]{:S(2)}) async-start(), calls=%async_computation.3 | async-start | bytes 3538944 | tf_op jit(solution)/shard_map/all_gather | solution.py:90
  61.1 3.9 copy-start.1
  71.9 1.4 copy-start.4
  74.9 3.5 copy-start.6
  78.4 29.7 %copy-start.11 = (u32[128]{0:T(128)S(1)}, u32[128]{0:T(128)}, u32[]{:S(2)}) copy-start(u32[128]{0:T(128)} %constant.56) | copy-start | bytes 1540
  78.4 126.0 %all-gather.9.cloned.1.call-start = ((), (), s32[]{:S(2)}) async-start(), calls=%async_computation.6 | async-start | bytes 3538944 | tf_op jit(solution)/shard_map/all_gather | solution.py:91
  81.5 70.9 %copy-start.9 = (f32[64]{0:T(128)S(1)}, f32[64]{0:T(128)}, u32[]{:S(2)}) copy-start(f32[64]{0:T(128)} %param.21) | copy-start | bytes 772
  152.2 116.5 %reduce-scatter.3.cloned.1.call-start = ((), (), s32[]{:S(2)}) async-start(), calls=%async_computation.4 | async-start | bytes 3112960 | tf_op jit(solution)/shard_map/reduce_scatter | solution.py:132
  204.4 19.9 %copy-start.3 = (f32[6,512,160]{1,2,0:T(8,128)S(1)}, f32[6,512,160]{1,2,0:T(8,128)}, u32[]{:S(2)}) copy-start(f32[6,512,160]{1,2,0:T(8,128)} %get-tuple-element.21) | copy-start | bytes 5898244
  204.4 19.9 %copy-start.7 = (bf16[1,160,1,384]{1,3,2,0:T(8,128)(2,1)S(1)}, bf16[1,160,1,384]{1,3,2,0:T(8,128)(2,1)}, u32[]{:S(2)}) copy-start(bf16[1,160,1,384]{1,3,2,0:T(8,128)(2,1)} %copy.39) | copy-start | bytes 368644
  224.3 1.5 copy-start.5
  228.8 123.5 %all-gather.11.cloned.1.call-start = ((), (), s32[]{:S(2)}) async-start(), calls=%async_computation.7 | async-start | bytes 10584064 | tf_op jit(solution)/shard_map/all_gather | solution.py:147
  270.3 0.8 copy-start.2
  272.4 206.6 %reduce-scatter.5.cloned.1.call-start = ((), (), s32[]{:S(2)}) async-start(), calls=%async_computation.5 | async-start | bytes 10584064 | tf_op jit(solution)/shard_map/reduce_scatter | solution.py:154
Sparse Core Ops, SparseCore 0:
  78.5 45.3 all-gather.6
  152.3 52.0 all-gather.8
  228.9 39.7 reduce-scatter.2
  272.5 79.7 all-gather.10
  373.0 105.9 reduce-scatter.4
